TPU v7x, 128 devices: a whole 4x4x4 slice. The times are simulated.
128 devices in a mesh: req: 16 (over x, y), kv: 8 (over z, core).
Axes of the slice: x: 4, y: 4, z: 4, core: 2. Of those that a mesh axis runs over, the one named last changes fastest.
Arguments:
- hidden: bfloat16 [1024, 2048], P('req', 'kv'), may hold values from -6 to 6
- attn_gain: float32 [2048], replicated, may hold values from 0.25 to 1.75
- q_gain: float32 [128], replicated, may hold values from 0.25 to 1.75
- k_gain: float32 [128], replicated, may hold values from 0.25 to 1.75
- w_q: bfloat16 [2048, 2048], P(None, 'kv'), may hold values from -0.125 to 0.125
- w_gate_attn: bfloat16 [2048, 2048], P(None, 'kv'), may hold values from -0.125 to 0.125
- w_k: bfloat16 [2048, 1024], P(None, 'kv'), may hold values from -0.125 to 0.125
- w_v: bfloat16 [2048, 1024], P(None, 'kv'), may hold values from -0.125 to 0.125
- w_o: bfloat16 [2048, 2048], P('kv'), may hold values from -0.125 to 0.125
- k_pool: bfloat16 [2784, 128, 1024], P('req', None, 'kv'), may hold values from -245 to 245
- v_pool: bfloat16 [2784, 128, 1024], P('req', None, 'kv'), may hold values from -6 to 6
- lengths: int32 [1024], P('req'), may hold values from 1 to 4095, as said below
- page_table: int32 [1024, 32], P('req'), may hold values from 0 to 173, as said below
- mig_request: int32 [16, 16], P('req'), may hold values from 0 to 63, as said below
- mig_dest: int32 [16, 16], P('req'), may hold values from 0 to 15, as said below
- mlp_gain: float32 [2048], replicated, may hold values from 0.25 to 1.75
- w_gate: bfloat16 [2048, 6144], P(None, ('req', 'kv')), may hold values from -0.125 to 0.125
- w_up: bfloat16 [2048, 6144], P(None, ('req', 'kv')), may hold values from -0.125 to 0.125
- w_down: bfloat16 [2048, 6144], P(None, ('req', 'kv')), may hold values from -0.078125 to 0.078125
Outputs:
- out_hidden: bfloat16 [1024, 2048], P('req', 'kv')
- mig_keys: bfloat16 [256, 512, 1024], P('req', None, 'kv')
- mig_values: bfloat16 [256, 512, 1024], P('req', None, 'kv')
Inputs may be any that keep to these rules, and one draw needn't show every extreme that they name: lengths[r] tokens of request r are cached and its new token takes position lengths[r]; some request holds 4095 cached tokens. `page_table`: entries refer to the pool of the request's own device. The first lengths[r] // 128 + 1 entries of row r are the request's pages, distinct and never shared with another request of that device; later entries are valid pages that are not read. `mig_request`: row s names 16 different requests of device s; each has at most 511 cached tokens, and in every row one has exactly that many. `mig_dest`: each row is a permutation.
All inputs are finite; a program needn't handle non-finite values.
Results may differ from a plain program's by a relative error of at most 0.0093.
Values may be sent and summed in bfloat16 or wider, within the bound.
No kernel may reach another device: no remote copies, remote signals or barrier semaphores. Data moves between devices by JAX's collectives and lax.ppermute only.
A program may use at most 128 MiB of HBM per device.

v0:
```python
import jax
import jax.numpy as jnp
from jax import lax
from jax.sharding import PartitionSpec as P

MIGP = 4
EPSILON = 1e-06
ROPE_BASE = 1000000.0


def rms_norm(values, scale_row):
    values = values.astype(jnp.float32)
    return (
        values * lax.rsqrt(jnp.mean(values * values, axis=-1, keepdims=True) + EPSILON) * scale_row
    )


def rotate(values, position):
    half_dim = values.shape[-1] // 2
    frequency = ROPE_BASE ** (-jnp.arange(half_dim, dtype=jnp.float32) * 2.0 / values.shape[-1])
    angles = position.astype(jnp.float32)[:, None, None] * frequency
    cosine = jnp.cos(angles)
    sine_part = jnp.sin(angles)
    first_half = values[..., :half_dim]
    second = values[..., half_dim:]
    return jnp.concatenate(
        [first_half * cosine - second * sine_part, second * cosine + first_half * sine_part],
        axis=-1,
    )


def attend_pool(queries, new_keys, new_values, k_pool, v_pool, lengths, page_table):
    req_count, kv_local, group_size, head_dim = queries.shape
    pool_pages, page_size, _ = k_pool.shape
    table_width = page_table.shape[1]
    token_count = pool_pages * page_size
    score_scale = head_dim ** (-0.5)
    slot_ids = jnp.arange(table_width, dtype=jnp.int32)
    in_use = slot_ids[None, :] < (lengths // page_size + 1)[:, None]
    targets = jnp.where(in_use, page_table, pool_pages).reshape(-1)
    owner = (
        jnp.full((pool_pages,), -1, jnp.int32)
        .at[targets]
        .set(jnp.repeat(jnp.arange(req_count, dtype=jnp.int32), table_width), mode="drop")
    )
    first_pos = (
        jnp.zeros((pool_pages,), jnp.int32)
        .at[targets]
        .set(jnp.tile(slot_ids * page_size, req_count), mode="drop")
    )
    token_owner = jnp.repeat(owner, page_size)
    token_pos = (first_pos[:, None] + jnp.arange(page_size, dtype=jnp.int32)[None, :]).reshape(-1)
    valid = (token_owner[None, :] == jnp.arange(req_count, dtype=jnp.int32)[:, None]) & (
        token_pos[None, :] < lengths[:, None]
    )
    keys = k_pool.reshape(token_count, kv_local, head_dim)
    values = v_pool.reshape(token_count, kv_local, head_dim)
    scores = (
        jnp.einsum("rkgd,tkd->rkgt", queries, keys, preferred_element_type=jnp.float32)
        * score_scale
    )
    scores = jnp.where(valid[:, None, None, :], scores, -jnp.inf)
    own_score = (
        jnp.einsum("rkgd,rkd->rkg", queries, new_keys, preferred_element_type=jnp.float32)
        * score_scale
    )
    row_top = jnp.maximum(jnp.max(scores, axis=-1), own_score)
    exps_all = jnp.exp(scores - row_top[..., None])
    own_exp = jnp.exp(own_score - row_top)
    denom_sum = jnp.sum(exps_all, axis=-1) + own_exp
    weights = (exps_all / denom_sum[..., None]).astype(jnp.bfloat16)
    own_weight = (own_exp / denom_sum).astype(jnp.bfloat16)
    start_sum = jnp.einsum(
        "rkg,rkd->rkgd", own_weight, new_values, preferred_element_type=jnp.float32
    )
    return start_sum + jnp.einsum(
        "rkgt,tkd->rkgd", weights, values, preferred_element_type=jnp.float32
    )


def reduce_to_slice(partial, kv_count, slice_width):
    rows = partial.shape[0]
    pieces = partial.reshape(rows, kv_count, slice_width).transpose(1, 0, 2)
    arrived = lax.all_to_all(pieces, "kv", 0, 0, tiled=True)
    return jnp.sum(arrived, axis=0)


def per_device(
    hidden,
    attn_gain,
    q_gain,
    k_gain,
    w_q,
    w_gate_attn,
    w_k,
    w_v,
    w_o,
    k_pool,
    v_pool,
    lengths,
    page_table,
    mig_request,
    mig_dest,
    mlp_gain,
    w_gate,
    w_up,
    w_down,
):
    head_dim = q_gain.shape[0]
    req_count = hidden.shape[0]
    kv_local = w_k.shape[1] // head_dim
    q_local = w_q.shape[1] // head_dim
    group_size = q_local // kv_local
    page_size = k_pool.shape[1]
    channels = kv_local * head_dim
    model_width = mlp_gain.shape[0]
    gate_w = lax.all_gather(w_gate, "req", axis=1, tiled=True)
    up_w = lax.all_gather(w_up, "req", axis=1, tiled=True)
    down_w = lax.all_gather(w_down, "req", axis=1, tiled=True)
    whole_rows = lax.all_gather(hidden, "kv", axis=1, tiled=True)
    normed = rms_norm(whole_rows, attn_gain).astype(jnp.bfloat16)
    query_raw = jnp.dot(normed, w_q, preferred_element_type=jnp.float32).reshape(
        req_count, q_local, head_dim
    )
    gate_raw = jnp.dot(normed, w_gate_attn, preferred_element_type=jnp.float32)
    key_raw = jnp.dot(normed, w_k, preferred_element_type=jnp.float32).reshape(
        req_count, kv_local, head_dim
    )
    value_raw = jnp.dot(normed, w_v, preferred_element_type=jnp.float32).reshape(
        req_count, kv_local, head_dim
    )
    queries = rotate(rms_norm(query_raw, q_gain), lengths).astype(jnp.bfloat16)
    queries = queries.reshape(req_count, kv_local, group_size, head_dim)
    new_keys = rotate(rms_norm(key_raw, k_gain), lengths).astype(jnp.bfloat16)
    new_values = value_raw.astype(jnp.bfloat16)
    mig_rows = mig_request[0]
    dest_row = mig_dest[0]
    mig_count = mig_rows.shape[0]
    slot_count = MIGP * page_size
    moved_pages = page_table[mig_rows, :MIGP]
    slot_pos = jnp.arange(slot_count, dtype=jnp.int32)[None, :, None]
    moved_len = lengths[mig_rows][:, None, None]
    zero_value = jnp.zeros((), jnp.bfloat16)
    inverse = jnp.zeros_like(dest_row).at[dest_row].set(jnp.arange(mig_count, dtype=jnp.int32))

    def place_cache(pool, fresh_rows):
        cached = pool[moved_pages].reshape(mig_count, slot_count, channels)
        fresh_row = fresh_rows.reshape(req_count, channels)[mig_rows][:, None, :]
        filled = jnp.where(
            slot_pos < moved_len, cached, jnp.where(slot_pos == moved_len, fresh_row, zero_value)
        )
        return filled[inverse]

    mig_keys, mig_values = (
        lax.all_to_all(
            place_cache(k_pool, new_keys), "req", split_axis=0, concat_axis=0, tiled=True
        ),
        lax.all_to_all(
            place_cache(v_pool, new_values), "req", split_axis=0, concat_axis=0, tiled=True
        ),
    )
    context = attend_pool(queries, new_keys, new_values, k_pool, v_pool, lengths, page_table)
    gated = (jax.nn.sigmoid(gate_raw) * context.reshape(req_count, q_local * head_dim)).astype(
        jnp.bfloat16
    )
    head_terms = jnp.dot(gated, w_o, preferred_element_type=jnp.float32)
    kv_count = lax.axis_size("kv")
    slice_width = model_width // kv_count
    mid_slice = (
        hidden.astype(jnp.float32) + reduce_to_slice(head_terms, kv_count, slice_width)
    ).astype(jnp.bfloat16)
    mid_stream = lax.all_gather(mid_slice, "kv", axis=1, tiled=True)
    normed_mlp = rms_norm(mid_stream, mlp_gain).astype(jnp.bfloat16)
    gate_part = jnp.dot(normed_mlp, gate_w, preferred_element_type=jnp.float32)
    up_part = jnp.dot(normed_mlp, up_w, preferred_element_type=jnp.float32)
    activation = (jax.nn.silu(gate_part) * up_part).astype(jnp.bfloat16)
    down_part = jnp.einsum("ru,cu->rc", activation, down_w, preferred_element_type=jnp.float32)
    mlp_part = reduce_to_slice(down_part, kv_count, slice_width)
    out_hidden = (mid_slice.astype(jnp.float32) + mlp_part).astype(jnp.bfloat16)
    return (out_hidden, mig_keys, mig_values)


def solution(mesh):
    return jax.shard_map(
        per_device,
        mesh=mesh,
        in_specs=(
            P("req", "kv"),
            P(),
            P(),
            P(),
            P(None, "kv"),
            P(None, "kv"),
            P(None, "kv"),
            P(None, "kv"),
            P("kv", None),
            P("req", None, "kv"),
            P("req", None, "kv"),
            P("req"),
            P("req", None),
            P("req", None),
            P("req", None),
            P(),
            P(None, ("req", "kv")),
            P(None, ("req", "kv")),
            P(None, ("req", "kv")),
        ),
        out_specs=(P("req", "kv"), P("req", None, "kv"), P("req", None, "kv")),
        check_vma=False,
    )
```

profile of v0, /device:TPU:1, one launch (start us, length us, event | category | flops | bytes accessed | tf_op | source)
XLA Modules:
  0.0 233.5 jit_solution(11153392332926695177)
XLA Ops:
  8.7 15.6 %all_gather.15 = bf16[64,2048]{1,0:T(8,128)(2,1)S(1)} all-gather(bf16[64,256]{1,0:T(8,128)(2,1)} %param.19), channel_id=1, replica_groups=mesh['req'=16,'kv'=8] {'kv'}, dimensions={1}, use_global_device_ids=true | all-gather | bytes 294912 | tf_op jit(solution)/shard_map/all_gather | solution.py:120
  24.5 1.6 fusion.71
  28.9 8.0 %scatter_custom_fusion.1 = s32[174]{0:T(256)S(1)} fusion(s32[2048]{0:T(1024)S(1)} %bitcast.141, s32[2048]{0:T(1024)S(1)} %reshape.579, s32[]{:T(128)} %constant.29.clone.1), kind=kCustom, calls=%fused_computation.124 | custom fusion | bytes 700 | tf_op jit(solution)/shard_map/scatter | solution.py:49
  37.0 8.0 %scatter_custom_fusion = s32[174]{0:T(256)S(1)} fusion(s32[2048]{0:T(1024)S(1)} %bitcast.142, s32[2048]{0:T(1024)S(1)} %reshape.571, s32[]{:T(128)} %constant.27.clone.1), kind=kCustom, calls=%fused_computation.127 | custom fusion | bytes 700 | tf_op jit(solution)/shard_map/scatter | solution.py:44
  47.4 4.3 %fusion.75 = (f32[64,2]{0,1:T(2,128)S(1)}, f32[64,1,2,22272]{3,0,2,1:T(8,128)S(1)}) fusion(bf16[64,2,128]{2,0,1:T(8,128)(2,1)S(1)} %pad_maximum_fusion, bf16[22272,128,1]{1,0,2:T(8,128)(2,1)} %bitcast.133, pred[64,22272]{1,0:T(8,128)(4,1)S(1)} %fusion.5), kind=kOutput, calls=%fused_computation.141 | convolution fusion | flops 738361216 | bytes 18563584 | tf_op jit(solution)/shard_map/rkgd,tkd->rkgt/dot_general | solution.py:59
  51.8 2.3 fusion.2
  54.4 5.4 %fusion.15 = f32[64,1,2,128]{3,0,2,1:T(8,128)S(1)} fusion(bf16[22272,128,1]{1,0,2:T(8,128)(2,1)} %bitcast.139, f32[64,2]{0,1:T(2,128)S(1)} %get-tuple-element.12, f32[64,1,2,22272]{3,0,2,1:T(8,128)S(1)} %get-tuple-element.26, f32[64,2]{0,1:T(2,128)S(1)} %fusion.54, f32[64,128]{1,0:T(8,128)S(1)} %get-tuple-element.27, f32[64,2]{0,1:T(2,128)S(1)} %get-tuple-element.11), kind=kOutput, calls=%fused_computation.35 | convolution fusion | flops 738394112 | bytes 17204736 | tf_op jit(solution)/shard_map/rkgt,tkd->rkgd/dot_general | solution.py:76
  59.8 2.1 fusion.19
  62.7 4.3 %all-to-all-start = ((f32[8,64,256]{2,1,0:T(8,128)}), f32[8,64,256]{2,1,0:T(8,128)}, u32[]{:S(2)}, u32[]{:S(2)}) async-start(f32[8,64,256]{2,1,0:T(8,128)} %bitcast.131), calls=%async_computation | async-start | bytes 1048576 | tf_op jit(solution)/shard_map/all_to_all | solution.py:84
  70.8 3.7 %gather_fusion.4 = bf16[64,128,128]{2,1,0:T(8,128)(2,1)S(1)} fusion(bf16[174,128,128]{2,1,0:T(8,128)(2,1)} %param.29, s32[1024]{0:T(1024)S(1)} %pad_clamp_fusion.1), kind=kCustom, calls=%fused_computation.4 | custom fusion | bytes 4194560 | tf_op jit(solution)/shard_map/gather | solution.py:147
  74.5 4.8 %gather_fusion.1 = bf16[64,128,128]{2,1,0:T(8,128)(2,1)} fusion(bf16[174,128,128]{2,1,0:T(8,128)(2,1)} %param.28, s32[1024]{0:T(1024)S(1)} %pad_clamp_fusion.1), kind=kCustom, calls=%fused_computation.1 | custom fusion | bytes 4194560 | tf_op jit(solution)/shard_map/gather | solution.py:147
  82.0 7.2 %bitcast_select_fusion = (bf16[16,512,128]{2,1,0:T(8,128)(2,1)}, bf16[16,512,128]{2,1,0:T(8,128)(2,1)}) fusion(pred[16,512]{1,0:T(8,128)(4,1)S(1)} %get-tuple-element.18, pred[16,512]{1,0:T(8,128)(4,1)S(1)} %get-tuple-element.17, bf16[16,128]{1,0:T(8,128)(2,1)S(1)} %gather_fusion.5, bf16[16,128]{1,0:T(8,128)(2,1)S(1)} %gather_fusion.2, ...), kind=kLoop, calls=%fused_computation.24 | loop fusion | flops 4194304 | bytes 8413184 | tf_op jit(solution)/shard_map/jit(_where)/select_n | solution.py:149
  89.2 3.9 %gather_fusion.3 = bf16[16,512,128]{2,1,0:T(8,128)(2,1)} fusion(bf16[16,512,128]{2,1,0:T(8,128)(2,1)} %get-tuple-element.10, s32[1024]{0:T(1024)S(1)} %pad_clamp_fusion), kind=kCustom, calls=%fused_computation.3 | custom fusion | bytes 4194368 | tf_op jit(solution)/shard_map/gather | solution.py:152
  93.0 7.0 %all-to-all-start.2 = ((bf16[16,512,128]{2,1,0:T(8,128)(2,1)}), bf16[16,512,128]{2,1,0:T(8,128)(2,1)}, u32[]{:S(2)}, u32[]{:S(2)}) async-start(bf16[16,512,128]{2,1,0:T(8,128)(2,1)} %gather_fusion.3), calls=%async_computation.2 | async-start | bytes 4194304 | tf_op jit(solution)/shard_map/all_to_all | solution.py:155
  100.0 2.1 gather_fusion.6
  102.2 32.1 %all-to-all-done.2 = bf16[16,512,128]{2,1,0:T(8,128)(2,1)} async-done(((bf16[16,512,128]{2,1,0:T(8,128)(2,1)}), bf16[16,512,128]{2,1,0:T(8,128)(2,1)}, u32[]{:S(2)}, u32[]{:S(2)}) %all-to-all-start.2) | async-done | bytes 2097184 | tf_op jit(solution)/shard_map/all_to_all | solution.py:155
  134.3 7.8 %all-to-all-start.3 = ((bf16[16,512,128]{2,1,0:T(8,128)(2,1)}), bf16[16,512,128]{2,1,0:T(8,128)(2,1)S(1)}, u32[]{:S(2)}, u32[]{:S(2)}) async-start(bf16[16,512,128]{2,1,0:T(8,128)(2,1)} %gather_fusion.6), calls=%async_computation.3 | async-start | bytes 4194304 | tf_op jit(solution)/shard_map/all_to_all | solution.py:158
  143.2 14.0 %all_gather.16 = bf16[64,2048]{1,0:T(8,128)(2,1)S(1)} all-gather(bf16[64,256]{1,0:T(8,128)(2,1)S(1)} %add_convert_fusion.1), channel_id=1, replica_groups=mesh['req'=16,'kv'=8] {'kv'}, dimensions={1}, use_global_device_ids=true | all-gather | bytes 294912 | tf_op jit(solution)/shard_map/all_gather | solution.py:172
  157.4 3.7 %fusion.34 = f32[64,768]{1,0:T(8,128)} fusion(bf16[2048,768]{0,1:T(8,128)(2,1)} %all-gather.4.cloned.1.call-done, bf16[64,2048]{1,0:T(8,128)(2,1)S(1)} %all_gather.16, f32[2048]{0:T(1024)S(1)} %copy-done.7, f32[64]{0:T(128)S(1)} %add_rsqrt_fusion.1), kind=kOutput, calls=%fused_computation.58 | convolution fusion | flops 201850880 | bytes 3612928 | tf_op jit(solution)/shard_map/dot_general | solution.py:174
  161.0 36.9 %all-gather.8.cloned.1.call-done = bf16[2048,768]{0,1:T(8,128)(2,1)} async-done(((bf16[2048,48]{0,1:T(8,128)(2,1)}), bf16[2048,768]{0,1:T(8,128)(2,1)}) %all-gather.8.cloned.1.call-update) | async-done | bytes 3145744 | tf_op jit(solution)/shard_map/all_gather | solution.py:119
  197.9 5.9 %fusion.7 = f32[64,2048]{1,0:T(8,128)} fusion(bf16[2048,768]{0,1:T(8,128)(2,1)} %all-gather.8.cloned.1.call-done, bf16[2048,768]{0,1:T(8,128)(2,1)} %all-gather.6.cloned.1.call-done, f32[64,768]{1,0:T(8,128)} %fusion.34, bf16[64,2048]{1,0:T(8,128)(2,1)S(1)} %all_gather.16, f32[2048]{0:T(1024)S(1)} %copy-done.7, f32[64]{0:T(128)S(1)} %add_rsqrt_fusion.1), kind=kOutput, calls=%fused_computation.28 | convolution fusion | flops 403472384 | bytes 7282944 | tf_op jit(solution)/shard_map/ru,cu->rc/dot_general | solution.py:177
  203.8 1.9 copy.60
  205.7 15.1 %all_to_all.20 = f32[8,64,256]{2,1,0:T(8,128)} all-to-all(f32[8,64,256]{2,1,0:T(8,128)} %bitcast.138), channel_id=1, replica_groups=mesh['req'=16,'kv'=8] {'kv'}, dimensions={0} | all-to-all | bytes 1048576 | tf_op jit(solution)/shard_map/all_to_all | solution.py:84
  222.5 3.1 %copy.64 = bf16[16,512,128]{2,1,0:T(8,128)(2,1)} copy(bf16[16,512,128]{2,1,0:T(8,128)(2,1)} %all-to-all-done.2) | data formatting | bytes 4194304
  (102 shorter events, 18.6 us)
Async XLA Ops:
  7.2 52.6 %copy-start = (bf16[256,2048]{1,0:T(8,128)(2,1)S(1)}, bf16[256,2048]{1,0:T(8,128)(2,1)}, u32[]{:S(2)}) copy-start(bf16[256,2048]{1,0:T(8,128)(2,1)} %param.27) | copy-start | bytes 3145732
  7.2 37.9 %copy-start.1 = (s32[64]{0:T(128)S(1)}, s32[64]{0:T(128)}, u32[]{:S(2)}) copy-start(s32[64]{0:T(128)} %param.30) | copy-start | bytes 772
  7.2 21.4 %copy-start.2 = (s32[64,32]{0,1:T(8,128)S(1)}, s32[64,32]{0,1:T(8,128)}, u32[]{:S(2)}) copy-start(s32[64,32]{0,1:T(8,128)} %param.31) | copy-start | bytes 24580
  7.2 39.1 %copy-start.8 = (f32[128]{0:T(128)S(1)}, f32[128]{0:T(128)}, u32[]{:S(2)}) copy-start(f32[128]{0:T(128)} %param.22) | copy-start | bytes 1540
  7.2 39.7 %copy-start.9 = (f32[128]{0:T(128)S(1)}, f32[128]{0:T(128)}, u32[]{:S(2)}) copy-start(f32[128]{0:T(128)} %param.21) | copy-start | bytes 1540
  7.2 150.1 %all-gather.4.cloned.1.call-start = ((), (), s32[]{:S(2)}) async-start(), calls=%async_computation.4 | async-start | bytes 3342336 | tf_op jit(solution)/shard_map/all_gather | solution.py:117
  8.0 153.1 %all-gather.6.cloned.1.call-start = ((), (), s32[]{:S(2)}) async-start(), calls=%async_computation.5 | async-start | bytes 3342336 | tf_op jit(solution)/shard_map/all_gather | solution.py:118
  51.7 2.3 copy-start.4
  51.8 2.3 copy-start.6
  59.7 8.0 %copy-start.11 = (s32[1,16]{1,0:T(1,128)S(1)}, s32[1,16]{1,0:T(1,128)}, u32[]{:S(2)}) copy-start(s32[1,16]{1,0:T(1,128)} %param.32) | copy-start | bytes 196
  59.7 8.1 %copy-start.10 = (s32[2]{0:T(128)S(1)}, s32[2]{0:T(128)}, u32[]{:S(2)}) copy-start(s32[2]{0:T(128)} %constant.75) | copy-start | bytes 28
  62.7 30.3 %all-to-all-start = ((f32[8,64,256]{2,1,0:T(8,128)}), f32[8,64,256]{2,1,0:T(8,128)}, u32[]{:S(2)}, u32[]{:S(2)}) async-start(f32[8,64,256]{2,1,0:T(8,128)} %bitcast.131), calls=%async_computation | async-start | bytes 1048576 | tf_op jit(solution)/shard_map/all_to_all | solution.py:84
  67.0 130.9 %all-gather.8.cloned.1.call-start = ((), (), s32[]{:S(2)}) async-start(), calls=%async_computation.6 | async-start | bytes 3342336 | tf_op jit(solution)/shard_map/all_gather | solution.py:119
  74.5 6.7 %copy-start.12 = (s32[1,16]{1,0:T(1,128)S(1)}, s32[1,16]{1,0:T(1,128)}, u32[]{:S(2)}) copy-start(s32[1,16]{1,0:T(1,128)} %param.33) | copy-start | bytes 196
  93.0 7.0 %copy-start.3 = (bf16[16,512,128]{2,1,0:T(8,128)(2,1)S(1)}, bf16[16,512,128]{2,1,0:T(8,128)(2,1)}, u32[]{:S(2)}) copy-start(bf16[16,512,128]{2,1,0:T(8,128)(2,1)} %get-tuple-element.9) | copy-start | bytes 6291460
  93.0 41.3 %all-to-all-start.2 = ((bf16[16,512,128]{2,1,0:T(8,128)(2,1)}), bf16[16,512,128]{2,1,0:T(8,128)(2,1)}, u32[]{:S(2)}, u32[]{:S(2)}) async-start(bf16[16,512,128]{2,1,0:T(8,128)(2,1)} %gather_fusion.3), calls=%async_computation.2 | async-start | bytes 4194304 | tf_op jit(solution)/shard_map/all_to_all | solution.py:155
  102.2 41.0 %copy-start.5 = (bf16[64,256]{1,0:T(8,128)(2,1)S(1)}, bf16[64,256]{1,0:T(8,128)(2,1)}, u32[]{:S(2)}) copy-start(bf16[64,256]{1,0:T(8,128)(2,1)} %param.19) | copy-start | bytes 98308
  102.2 55.2 %copy-start.7 = (f32[2048]{0:T(1024)S(1)}, f32[2048]{0:T(1024)}, u32[]{:S(2)}) copy-start(f32[2048]{0:T(1024)} %param.34) | copy-start | bytes 24580
  134.3 71.4 %all-to-all-start.3 = ((bf16[16,512,128]{2,1,0:T(8,128)(2,1)}), bf16[16,512,128]{2,1,0:T(8,128)(2,1)S(1)}, u32[]{:S(2)}, u32[]{:S(2)}) async-start(bf16[16,512,128]{2,1,0:T(8,128)(2,1)} %gather_fusion.6), calls=%async_computation.3 | async-start | bytes 4194304 | tf_op jit(solution)/shard_map/all_to_all | solution.py:158
Sparse Core Ops, SparseCore 0:
  10.2 50.2 all-gather.3
  62.7 59.2 all-gather.5
  124.2 73.6 all-gather.7
where the time goes:
time: 234 us; the launch traced here: 233 us
  waiting for transfers between devices  71.1 us (30%)
  blocking collectives  44.7 us (19%)
  local copies, waits for them, and re-layouts  43.6 us (19%)
  matrix products  24.7 us (11%)
  starting transfers between devices  19.2 us (8%)
  other arithmetic  16 us (7%)
  between operations  14.2 us (6%)
    all_gather x1, waiting for transfers between devices, per_device(): down_w = lax.all_gather(w_down, 'req', axis=1, tiled=True)  36.9 us
    all_to_all x1, waiting for transfers between devices, per_device(): lax.all_to_all(place_cache(k_pool, new_keys), 'req', split_axis=0, concat...  32.1 us
    all_gather x1, blocking collectives, per_device(): whole_rows = lax.all_gather(hidden, 'kv', axis=1, tiled=True)  15.6 us
    all_to_all x1, blocking collectives, reduce_to_slice(): arrived = lax.all_to_all(pieces, 'kv', 0, 0, tiled=True)  15.1 us
    all_gather x1, blocking collectives, per_device(): mid_stream = lax.all_gather(mid_slice, 'kv', axis=1, tiled=True)  14 us
    gather x2, local copies, waits for them, and re-layouts, place_cache(): cached = pool[moved_pages].reshape(mig_count, slot_count, channels)  8.49 us
    scatter x1, local copies, waits for them, and re-layouts, attend_pool(): first_pos = jnp.zeros((pool_pages,), jnp.int32).at[targets].set(jnp.tile(...  8.04 us
    scatter x1, local copies, waits for them, and re-layouts, attend_pool(): owner = jnp.full((pool_pages,), -1, jnp.int32).at[targets].set(jnp.repeat...  8.04 us
  transfers between devices with their start and end apart: 6, of which 2 were waited for; matrix products, arithmetic and copies ran while one was open for 33% of the time, Pallas kernels for 0%

commit v1 on v0

--- a/solution.py
+++ b/solution.py
@@ -6,6 +6,28 @@
 MIGP = 4
 EPSILON = 1e-06
 ROPE_BASE = 1000000.0
+
+
+def in_order(pieces, dim):
+    pieces = jnp.moveaxis(pieces, 0, dim)
+    dims = pieces.shape
+    return pieces.reshape(*dims[:dim], dims[dim] * dims[dim + 1], *dims[dim + 2 :])
+
+
+def collect(value, axis, dim):
+    count = lax.axis_size(axis)
+    pairs = [(i, (i + 1) % count) for i in range(count)]
+    back = [(b, a) for a, b in pairs]
+    lower, upper = ([], [])
+    for step in range(count - 1):
+        if step % 2 == 0:
+            lower.append(lax.ppermute(lower[-1] if lower else value, axis, pairs))
+        else:
+            upper.append(lax.ppermute(upper[-1] if upper else value, axis, back))
+    parts = jnp.stack([*lower[::-1], value, *upper])
+    shift = lax.axis_index(axis) - len(lower)
+    parts = parts[(jnp.arange(count) - shift) % count]
+    return in_order(parts, dim)
 
 
 def rms_norm(values, scale_row):
@@ -116,7 +138,7 @@
     model_width = mlp_gain.shape[0]
     gate_w = lax.all_gather(w_gate, "req", axis=1, tiled=True)
     up_w = lax.all_gather(w_up, "req", axis=1, tiled=True)
-    down_w = lax.all_gather(w_down, "req", axis=1, tiled=True)
+    down_w = collect(w_down, "req", 1)
     whole_rows = lax.all_gather(hidden, "kv", axis=1, tiled=True)
     normed = rms_norm(whole_rows, attn_gain).astype(jnp.bfloat16)
     query_raw = jnp.dot(normed, w_q, preferred_element_type=jnp.float32).reshape(

time: 234 us -> 268 us (1.15)
  starting transfers between devices: 19.2 us -> 51.7 us
  local copies, waits for them, and re-layouts: 43.6 us -> 68.8 us
  waiting for transfers between devices: 71.1 us -> 46.4 us
  blocking collectives: 44.7 us -> 47.9 us
    ppermute x0 -> x15, waiting for transfers between devices: none -> 37.6 us  [the longest x7 27.7 us: collect(): upper.append(lax.ppermute(upper[-1] if upper else value, axis, back))]
    all_gather x1 -> x0, waiting for transfers between devices: 36.9 us -> none  [per_device(): down_w = lax.all_gather(w_down, 'req', axis=1, tiled=True)]
    ppermute x0 -> x15, starting transfers between devices: none -> 36.7 us  [the longest x7 34.5 us: collect(): upper.append(lax.ppermute(upper[-1] if upper else value, axis, back))]
    all_to_all x1, waiting for transfers between devices: 32.1 us -> 0.01 us  [per_device(): lax.all_to_all(place_cache(k_pool, new_keys), 'req', split_axis=0, concat...]
    unnamed x28 -> x60, local copies, waits for them, and re-layouts: 4.5 us -> 26.1 us
    all_to_all x1, waiting for transfers between devices: 0.01 us -> 8.07 us  [per_device(): lax.all_to_all(place_cache(v_pool, new_values), 'req', split_axis=0, conc...]
    all_to_all x1, starting transfers between devices: 7.78 us -> 4.44 us  [per_device(): lax.all_to_all(place_cache(v_pool, new_values), 'req', split_axis=0, conc...]
  transfers between devices with their start and end apart: 6 -> 20, of which waited for: 2 -> 6; matrix products, arithmetic and copies ran while one was open for 33% -> 37% of each run, Pallas kernels for 0% -> 0%
where the time goes in v1:
time: 268 us; the launch traced here: 267 us
  local copies, waits for them, and re-layouts  68.8 us (26%)
  starting transfers between devices  51.7 us (19%)
  blocking collectives  47.9 us (18%)
  waiting for transfers between devices  46.4 us (17%)
  matrix products  23.8 us (9%)
  between operations  14.6 us (5%)
  other arithmetic  13.9 us (5%)
    ppermute x7, starting transfers between devices, collect(): upper.append(lax.ppermute(upper[-1] if upper else value, axis, back))  34.5 us
    ppermute x7, waiting for transfers between devices, collect(): upper.append(lax.ppermute(upper[-1] if upper else value, axis, back))  27.7 us
    unnamed x60, local copies, waits for them, and re-layouts  26.1 us
    all_to_all x1, blocking collectives, reduce_to_slice(): arrived = lax.all_to_all(pieces, 'kv', 0, 0, tiled=True)  17.7 us
    all_gather x1, blocking collectives, per_device(): mid_stream = lax.all_gather(mid_slice, 'kv', axis=1, tiled=True)  15.1 us
    all_gather x1, blocking collectives, per_device(): whole_rows = lax.all_gather(hidden, 'kv', axis=1, tiled=True)  15.1 us
    ppermute x8, waiting for transfers between devices, collect(): lower.append(lax.ppermute(lower[-1] if lower else value, axis, pairs))  9.89 us
    gather x2, local copies, waits for them, and re-layouts, place_cache(): cached = pool[moved_pages].reshape(mig_count, slot_count, channels)  9.58 us
  transfers between devices with their start and end apart: 20, of which 6 were waited for; matrix products, arithmetic and copies ran while one was open for 37% of the time, Pallas kernels for 0%

profile of v1, /device:TPU:1, one launch (start us, length us, event | category | flops | bytes accessed | tf_op | source)
XLA Modules:
  0.0 267.2 jit_solution(13403678380837663358)
XLA Ops:
  13.2 15.1 %all_gather.12 = bf16[64,2048]{1,0:T(8,128)(2,1)S(1)} all-gather(bf16[64,256]{1,0:T(8,128)(2,1)} %param.19), channel_id=1, replica_groups=mesh['req'=16,'kv'=8] {'kv'}, dimensions={1}, use_global_device_ids=true | all-gather | bytes 294912 | tf_op jit(solution)/shard_map/all_gather | solution.py:142
  32.9 8.0 %scatter_custom_fusion.1 = s32[174]{0:T(256)S(1)} fusion(s32[2048]{0:T(1024)S(1)} %bitcast.179, s32[2048]{0:T(1024)S(1)} %reshape.636, s32[]{:T(128)} %constant.39.clone.1), kind=kCustom, calls=%fused_computation.150 | custom fusion | bytes 700 | tf_op jit(solution)/shard_map/scatter | solution.py:71
  41.0 8.2 %scatter_custom_fusion = s32[174]{0:T(256)S(1)} fusion(s32[2048]{0:T(1024)S(1)} %bitcast.180, s32[2048]{0:T(1024)S(1)} %reshape.628, s32[]{:T(128)} %constant.34.clone.1), kind=kCustom, calls=%fused_computation.153 | custom fusion | bytes 700 | tf_op jit(solution)/shard_map/scatter | solution.py:66
  51.6 4.3 %fusion.82 = (f32[64,2]{0,1:T(2,128)S(1)}, f32[64,1,2,22272]{3,0,2,1:T(8,128)S(1)}) fusion(bf16[64,2,128]{2,0,1:T(8,128)(2,1)S(1)} %pad_maximum_fusion, bf16[22272,128,1]{1,0,2:T(8,128)(2,1)} %bitcast.173, pred[64,22272]{1,0:T(8,128)(4,1)S(1)} %fusion.5), kind=kOutput, calls=%fused_computation.167 | convolution fusion | flops 738361216 | bytes 18563584 | tf_op jit(solution)/shard_map/rkgd,tkd->rkgt/dot_general | solution.py:81
  58.6 5.2 %fusion.20 = f32[64,1,2,128]{3,0,2,1:T(8,128)S(1)} fusion(bf16[22272,128,1]{1,0,2:T(8,128)(2,1)} %bitcast.177, f32[64,2]{0,1:T(2,128)S(1)} %get-tuple-element.12, f32[64,1,2,22272]{3,0,2,1:T(8,128)S(1)} %get-tuple-element.26, f32[64,2]{0,1:T(2,128)S(1)} %fusion.59, f32[64,128]{1,0:T(8,128)S(1)} %get-tuple-element.27, f32[64,2]{0,1:T(2,128)S(1)} %get-tuple-element.11), kind=kOutput, calls=%fused_computation.39 | convolution fusion | flops 738394112 | bytes 17204736 | tf_op jit(solution)/shard_map/rkgt,tkd->rkgd/dot_general | solution.py:98
  66.8 4.3 %all-to-all-start = ((f32[8,64,256]{2,1,0:T(8,128)}), f32[8,64,256]{2,1,0:T(8,128)S(1)}, u32[]{:S(2)}, u32[]{:S(2)}) async-start(f32[8,64,256]{2,1,0:T(8,128)} %bitcast.169), calls=%async_computation | async-start | bytes 1048576 | tf_op jit(solution)/shard_map/all_to_all | solution.py:106
  74.9 4.8 %gather_fusion.5 = bf16[64,128,128]{2,1,0:T(8,128)(2,1)} fusion(bf16[174,128,128]{2,1,0:T(8,128)(2,1)} %param.29, s32[1024]{0:T(1024)S(1)} %get-tuple-element.29), kind=kCustom, calls=%fused_computation.5 | custom fusion | bytes 4194560 | tf_op jit(solution)/shard_map/gather | solution.py:169
  79.7 4.8 %gather_fusion.2 = bf16[64,128,128]{2,1,0:T(8,128)(2,1)} fusion(bf16[174,128,128]{2,1,0:T(8,128)(2,1)} %param.28, s32[1024]{0:T(1024)S(1)} %get-tuple-element.29), kind=kCustom, calls=%fused_computation.2 | custom fusion | bytes 4194560 | tf_op jit(solution)/shard_map/gather | solution.py:169
  86.5 7.3 %bitcast_select_fusion = (bf16[16,512,128]{2,1,0:T(8,128)(2,1)S(1)}, bf16[16,512,128]{2,1,0:T(8,128)(2,1)}) fusion(pred[16,512]{1,0:T(8,128)(4,1)S(1)} %get-tuple-element.18, pred[16,512]{1,0:T(8,128)(4,1)S(1)} %get-tuple-element.17, bf16[16,128]{1,0:T(8,128)(2,1)S(1)} %gather_fusion.6, bf16[16,128]{1,0:T(8,128)(2,1)S(1)} %gather_fusion.3, ...), kind=kLoop, calls=%fused_computation.27 | loop fusion | flops 4194304 | bytes 8413184 | tf_op jit(solution)/shard_map/jit(_where)/select_n | solution.py:171
  97.9 4.8 %collective-permute-start.9 = (bf16[2048,48]{0,1:T(8,128)(2,1)S(1)}, bf16[2048,48]{0,1:T(8,128)(2,1)S(1)}, u32[]{:S(2)}, u32[]{:S(2)}) collective-permute-start(bf16[2048,48]{0,1:T(8,128)(2,1)S(1)} %collective-permute-done.8), channel_id=1, source_target_pairs={{8,0},{16,8},{24,16},{32,24},{40,32},{48,40},{56,48},{64,56},{72,6... | collective-permute-start | bytes 589832 | tf_op jit(solution)/shard_map/ppermute | solution.py:26
  112.2 4.8 %collective-permute-start.10 = (bf16[2048,48]{0,1:T(8,128)(2,1)S(1)}, bf16[2048,48]{0,1:T(8,128)(2,1)}, u32[]{:S(2)}, u32[]{:S(2)}) collective-permute-start(bf16[2048,48]{0,1:T(8,128)(2,1)S(1)} %collective-permute-done.9), channel_id=1, source_target_pairs={{8,0},{16,8},{24,16},{32,24},{40,32},{48,40},{56,48},{64,56},{72,6... | collective-permute-start | bytes 589832 | tf_op jit(solution)/shard_map/ppermute | solution.py:26
  120.0 6.2 %all-to-all-start.2 = ((bf16[16,512,128]{2,1,0:T(8,128)(2,1)}), bf16[16,512,128]{2,1,0:T(8,128)(2,1)S(1)}, u32[]{:S(2)}, u32[]{:S(2)}) async-start(bf16[16,512,128]{2,1,0:T(8,128)(2,1)} %gather_fusion.4), calls=%async_computation.2 | async-start | bytes 4194304 | tf_op jit(solution)/shard_map/all_to_all | solution.py:177
  126.3 4.8 %collective-permute-start.11 = (bf16[2048,48]{0,1:T(8,128)(2,1)}, bf16[2048,48]{0,1:T(8,128)(2,1)S(1)}, u32[]{:S(2)}, u32[]{:S(2)}) collective-permute-start(bf16[2048,48]{0,1:T(8,128)(2,1)} %collective-permute-done.10), channel_id=1, source_target_pairs={{8,0},{16,8},{24,16},{32,24},{40,32},{48,40},{56,48},{64,56},{72,6... | collective-permute-start | bytes 589832 | tf_op jit(solution)/shard_map/ppermute | solution.py:26
  131.1 23.6 %collective-permute-done.11 = bf16[2048,48]{0,1:T(8,128)(2,1)S(1)} collective-permute-done((bf16[2048,48]{0,1:T(8,128)(2,1)}, bf16[2048,48]{0,1:T(8,128)(2,1)S(1)}, u32[]{:S(2)}, u32[]{:S(2)}) %collective-permute-start.11) | collective-permute-done | bytes 196640 | tf_op jit(solution)/shard_map/ppermute | solution.py:26
  154.7 5.6 %collective-permute-start.12 = (bf16[2048,48]{0,1:T(8,128)(2,1)S(1)}, bf16[2048,48]{0,1:T(8,128)(2,1)S(1)}, u32[]{:S(2)}, u32[]{:S(2)}) collective-permute-start(bf16[2048,48]{0,1:T(8,128)(2,1)S(1)} %collective-permute-done.11), channel_id=1, source_target_pairs={{8,0},{16,8},{24,16},{32,24},{40,32},{48,40},{56,48},{64,56},{72,6... | collective-permute-start | bytes 589832 | tf_op jit(solution)/shard_map/ppermute | solution.py:26
  160.3 15.1 %all_gather.13 = bf16[64,2048]{1,0:T(8,128)(2,1)S(1)} all-gather(bf16[64,256]{1,0:T(8,128)(2,1)S(1)} %add_convert_fusion.1), channel_id=1, replica_groups=mesh['req'=16,'kv'=8] {'kv'}, dimensions={1}, use_global_device_ids=true | all-gather | bytes 294912 | tf_op jit(solution)/shard_map/all_gather | solution.py:194
  175.6 5.1 %collective-permute-start.13 = (bf16[2048,48]{0,1:T(8,128)(2,1)S(1)}, bf16[2048,48]{0,1:T(8,128)(2,1)}, u32[]{:S(2)}, u32[]{:S(2)}) collective-permute-start(bf16[2048,48]{0,1:T(8,128)(2,1)S(1)} %collective-permute-done.12), channel_id=1, source_target_pairs={{8,0},{16,8},{24,16},{32,24},{40,32},{48,40},{56,48},{64,56},{72,6... | collective-permute-start | bytes 589832 | tf_op jit(solution)/shard_map/ppermute | solution.py:26
  180.7 4.1 %collective-permute-done.13 = bf16[2048,48]{0,1:T(8,128)(2,1)} collective-permute-done((bf16[2048,48]{0,1:T(8,128)(2,1)S(1)}, bf16[2048,48]{0,1:T(8,128)(2,1)}, u32[]{:S(2)}, u32[]{:S(2)}) %collective-permute-start.13) | collective-permute-done | bytes 196640 | tf_op jit(solution)/shard_map/ppermute | solution.py:26
  184.8 5.6 %collective-permute-start.14 = (bf16[2048,48]{0,1:T(8,128)(2,1)}, bf16[2048,48]{0,1:T(8,128)(2,1)}, u32[]{:S(2)}, u32[]{:S(2)}) collective-permute-start(bf16[2048,48]{0,1:T(8,128)(2,1)} %collective-permute-done.13), channel_id=1, source_target_pairs={{8,0},{16,8},{24,16},{32,24},{40,32},{48,40},{56,48},{64,56},{72,6... | collective-permute-start | bytes 589832 | tf_op jit(solution)/shard_map/ppermute | solution.py:26
  205.0 4.4 %all-to-all-start.3 = ((bf16[16,512,128]{2,1,0:T(8,128)(2,1)}), bf16[16,512,128]{2,1,0:T(8,128)(2,1)}, u32[]{:S(2)}, u32[]{:S(2)}) async-start(bf16[16,512,128]{2,1,0:T(8,128)(2,1)} %gather_fusion.7), calls=%async_computation.3 | async-start | bytes 4194304 | tf_op jit(solution)/shard_map/all_to_all | solution.py:180
  218.9 3.8 %fusion.39 = f32[64,768]{1,0:T(8,128)} fusion(bf16[2048,768]{0,1:T(8,128)(2,1)} %all-gather.3.cloned.1.call-done, bf16[64,2048]{1,0:T(8,128)(2,1)S(1)} %all_gather.13, f32[2048]{0:T(1024)S(1)} %copy-done.15, f32[64]{0:T(128)S(1)} %add_rsqrt_fusion.1), kind=kOutput, calls=%fused_computation.77 | convolution fusion | flops 201850880 | bytes 3612928 | tf_op jit(solution)/shard_map/dot_general | solution.py:196
  222.7 4.9 %fusion.8 = f32[8,64,256]{2,1,0:T(8,128)} fusion(bf16[8,256,768]{1,0,2:T(8,128)(2,1)S(1)} %bitcast.172, bf16[2048,768]{0,1:T(8,128)(2,1)} %all-gather.5.cloned.1.call-done, f32[64,768]{1,0:T(8,128)} %fusion.39, bf16[64,2048]{1,0:T(8,128)(2,1)S(1)} %all_gather.13, f32[2048]{0:T(1024)S(1)} %copy-done.15, f32[64]{0:T(128)S(1)} %add_rsqrt_fusion.1), kind=kOutput, calls=%fused_computation.29 | convolution fusion | flops 403472384 | bytes 7282944 | tf_op jit(solution)/shard_map/ru,cu->rc/dot_general | solution.py:199
  227.6 8.1 %all-to-all-done.3 = bf16[16,512,128]{2,1,0:T(8,128)(2,1)} async-done(((bf16[16,512,128]{2,1,0:T(8,128)(2,1)}), bf16[16,512,128]{2,1,0:T(8,128)(2,1)}, u32[]{:S(2)}, u32[]{:S(2)}) %all-to-all-start.3) | async-done | bytes 2097184 | tf_op jit(solution)/shard_map/all_to_all | solution.py:180
  235.6 17.7 %all_to_all.20 = f32[8,64,256]{2,1,0:T(8,128)S(1)} all-to-all(f32[8,64,256]{2,1,0:T(8,128)} %fusion.8), channel_id=1, replica_groups=mesh['req'=16,'kv'=8] {'kv'}, dimensions={0} | all-to-all | bytes 1048576 | tf_op jit(solution)/shard_map/all_to_all | solution.py:106
  (165 shorter events, 71.9 us)
Async XLA Ops:
  7.2 56.7 %copy-start = (bf16[256,2048]{1,0:T(8,128)(2,1)S(1)}, bf16[256,2048]{1,0:T(8,128)(2,1)}, u32[]{:S(2)}) copy-start(bf16[256,2048]{1,0:T(8,128)(2,1)} %param.27) | copy-start | bytes 3145732
  7.2 43.9 %copy-start.17 = (f32[128]{0:T(128)S(1)}, f32[128]{0:T(128)}, u32[]{:S(2)}) copy-start(f32[128]{0:T(128)} %param.21) | copy-start | bytes 1540
  7.2 211.6 %all-gather.3.cloned.1.call-start = ((), (), s32[]{:S(2)}) async-start(), calls=%async_computation.4 | async-start | bytes 3342336 | tf_op jit(solution)/shard_map/all_gather | solution.py:139
  7.3 79.2 %collective-permute-start = (bf16[2048,48]{0,1:T(8,128)(2,1)}, bf16[2048,48]{0,1:T(8,128)(2,1)S(1)}, u32[]{:S(2)}, u32[]{:S(2)}) collective-permute-start(bf16[2048,48]{0,1:T(8,128)(2,1)} %param.37), channel_id=1, source_target_pairs={{0,8},{8,16},{16,24},{24,32},{32,40},{40,48},{48,56},{56,64},{64,7... | collective-permute-start | bytes 589832 | tf_op jit(solution)/shard_map/ppermute | solution.py:24
  9.5 88.5 %collective-permute-start.8 = (bf16[2048,48]{0,1:T(8,128)(2,1)}, bf16[2048,48]{0,1:T(8,128)(2,1)S(1)}, u32[]{:S(2)}, u32[]{:S(2)}) collective-permute-start(bf16[2048,48]{0,1:T(8,128)(2,1)} %param.37), channel_id=1, source_target_pairs={{8,0},{16,8},{24,16},{32,24},{40,32},{48,40},{56,48},{64,56},{72,6... | collective-permute-start | bytes 589832 | tf_op jit(solution)/shard_map/ppermute | solution.py:26
  66.8 53.2 %all-to-all-start = ((f32[8,64,256]{2,1,0:T(8,128)}), f32[8,64,256]{2,1,0:T(8,128)S(1)}, u32[]{:S(2)}, u32[]{:S(2)}) async-start(f32[8,64,256]{2,1,0:T(8,128)} %bitcast.169), calls=%async_computation | async-start | bytes 1048576 | tf_op jit(solution)/shard_map/all_to_all | solution.py:106
  71.1 151.6 %all-gather.5.cloned.1.call-start = ((), (), s32[]{:S(2)}) async-start(), calls=%async_computation.5 | async-start | bytes 3342336 | tf_op jit(solution)/shard_map/all_gather | solution.py:140
  86.4 10.8 %collective-permute-start.1 = (bf16[2048,48]{0,1:T(8,128)(2,1)S(1)}, bf16[2048,48]{0,1:T(8,128)(2,1)S(1)}, u32[]{:S(2)}, u32[]{:S(2)}) collective-permute-start(bf16[2048,48]{0,1:T(8,128)(2,1)S(1)} %collective-permute-done), channel_id=1, source_target_pairs={{0,8},{8,16},{16,24},{24,32},{32,40},{40,48},{48,56},{56,64},{64,7... | collective-permute-start | bytes 589832 | tf_op jit(solution)/shard_map/ppermute | solution.py:24
  97.2 8.9 %collective-permute-start.2 = (bf16[2048,48]{0,1:T(8,128)(2,1)S(1)}, bf16[2048,48]{0,1:T(8,128)(2,1)S(1)}, u32[]{:S(2)}, u32[]{:S(2)}) collective-permute-start(bf16[2048,48]{0,1:T(8,128)(2,1)S(1)} %collective-permute-done.1), channel_id=1, source_target_pairs={{0,8},{8,16},{16,24},{24,32},{32,40},{40,48},{48,56},{56,64},{64,7... | collective-permute-start | bytes 589832 | tf_op jit(solution)/shard_map/ppermute | solution.py:24
  97.9 14.2 %collective-permute-start.9 = (bf16[2048,48]{0,1:T(8,128)(2,1)S(1)}, bf16[2048,48]{0,1:T(8,128)(2,1)S(1)}, u32[]{:S(2)}, u32[]{:S(2)}) collective-permute-start(bf16[2048,48]{0,1:T(8,128)(2,1)S(1)} %collective-permute-done.8), channel_id=1, source_target_pairs={{8,0},{16,8},{24,16},{32,24},{40,32},{48,40},{56,48},{64,56},{72,6... | collective-permute-start | bytes 589832 | tf_op jit(solution)/shard_map/ppermute | solution.py:26
  106.2 13.8 %collective-permute-start.3 = (bf16[2048,48]{0,1:T(8,128)(2,1)S(1)}, bf16[2048,48]{0,1:T(8,128)(2,1)}, u32[]{:S(2)}, u32[]{:S(2)}) collective-permute-start(bf16[2048,48]{0,1:T(8,128)(2,1)S(1)} %collective-permute-done.2), channel_id=1, source_target_pairs={{0,8},{8,16},{16,24},{24,32},{32,40},{40,48},{48,56},{56,64},{64,7... | collective-permute-start | bytes 589832 | tf_op jit(solution)/shard_map/ppermute | solution.py:24
  112.2 48.2 %copy-start.10 = (bf16[2048,48]{0,1:T(8,128)(2,1)}, bf16[2048,48]{0,1:T(8,128)(2,1)S(1)}, u32[]{:S(2)}) copy-start(bf16[2048,48]{0,1:T(8,128)(2,1)S(1)} %collective-permute-done.9) | copy-start | bytes 589828
  112.2 14.1 %collective-permute-start.10 = (bf16[2048,48]{0,1:T(8,128)(2,1)S(1)}, bf16[2048,48]{0,1:T(8,128)(2,1)}, u32[]{:S(2)}, u32[]{:S(2)}) collective-permute-start(bf16[2048,48]{0,1:T(8,128)(2,1)S(1)} %collective-permute-done.9), channel_id=1, source_target_pairs={{8,0},{16,8},{24,16},{32,24},{40,32},{48,40},{56,48},{64,56},{72,6... | collective-permute-start | bytes 589832 | tf_op jit(solution)/shard_map/ppermute | solution.py:26
  120.0 11.0 %collective-permute-start.4 = (bf16[2048,48]{0,1:T(8,128)(2,1)}, bf16[2048,48]{0,1:T(8,128)(2,1)}, u32[]{:S(2)}, u32[]{:S(2)}) collective-permute-start(bf16[2048,48]{0,1:T(8,128)(2,1)} %collective-permute-done.3), channel_id=1, source_target_pairs={{0,8},{8,16},{16,24},{24,32},{32,40},{40,48},{48,56},{56,64},{64,7... | collective-permute-start | bytes 589832 | tf_op jit(solution)/shard_map/ppermute | solution.py:24
  120.0 85.0 %all-to-all-start.2 = ((bf16[16,512,128]{2,1,0:T(8,128)(2,1)}), bf16[16,512,128]{2,1,0:T(8,128)(2,1)S(1)}, u32[]{:S(2)}, u32[]{:S(2)}) async-start(bf16[16,512,128]{2,1,0:T(8,128)(2,1)} %gather_fusion.4), calls=%async_computation.2 | async-start | bytes 4194304 | tf_op jit(solution)/shard_map/all_to_all | solution.py:177
  126.2 74.4 %copy-start.7 = (bf16[2048,48]{0,1:T(8,128)(2,1)S(1)}, bf16[2048,48]{0,1:T(8,128)(2,1)}, u32[]{:S(2)}) copy-start(bf16[2048,48]{0,1:T(8,128)(2,1)} %param.37) | copy-start | bytes 589828
  126.3 28.4 %collective-permute-start.11 = (bf16[2048,48]{0,1:T(8,128)(2,1)}, bf16[2048,48]{0,1:T(8,128)(2,1)S(1)}, u32[]{:S(2)}, u32[]{:S(2)}) collective-permute-start(bf16[2048,48]{0,1:T(8,128)(2,1)} %collective-permute-done.10), channel_id=1, source_target_pairs={{8,0},{16,8},{24,16},{32,24},{40,32},{48,40},{56,48},{64,56},{72,6... | collective-permute-start | bytes 589832 | tf_op jit(solution)/shard_map/ppermute | solution.py:26
  131.0 29.3 %collective-permute-start.5 = (bf16[2048,48]{0,1:T(8,128)(2,1)}, bf16[2048,48]{0,1:T(8,128)(2,1)S(1)}, u32[]{:S(2)}, u32[]{:S(2)}) collective-permute-start(bf16[2048,48]{0,1:T(8,128)(2,1)} %collective-permute-done.4), channel_id=1, source_target_pairs={{0,8},{8,16},{16,24},{24,32},{32,40},{40,48},{48,56},{56,64},{64,7... | collective-permute-start | bytes 589832 | tf_op jit(solution)/shard_map/ppermute | solution.py:24
  154.7 20.9 %collective-permute-start.12 = (bf16[2048,48]{0,1:T(8,128)(2,1)S(1)}, bf16[2048,48]{0,1:T(8,128)(2,1)S(1)}, u32[]{:S(2)}, u32[]{:S(2)}) collective-permute-start(bf16[2048,48]{0,1:T(8,128)(2,1)S(1)} %collective-permute-done.11), channel_id=1, source_target_pairs={{8,0},{16,8},{24,16},{32,24},{40,32},{48,40},{56,48},{64,56},{72,6... | collective-permute-start | bytes 589832 | tf_op jit(solution)/shard_map/ppermute | solution.py:26
  160.3 20.4 %collective-permute-start.6 = (bf16[2048,48]{0,1:T(8,128)(2,1)S(1)}, bf16[2048,48]{0,1:T(8,128)(2,1)S(1)}, u32[]{:S(2)}, u32[]{:S(2)}) collective-permute-start(bf16[2048,48]{0,1:T(8,128)(2,1)S(1)} %collective-permute-done.5), channel_id=1, source_target_pairs={{0,8},{8,16},{16,24},{24,32},{32,40},{40,48},{48,56},{56,64},{64,7... | collective-permute-start | bytes 589832 | tf_op jit(solution)/shard_map/ppermute | solution.py:24
  175.6 9.2 %collective-permute-start.13 = (bf16[2048,48]{0,1:T(8,128)(2,1)S(1)}, bf16[2048,48]{0,1:T(8,128)(2,1)}, u32[]{:S(2)}, u32[]{:S(2)}) collective-permute-start(bf16[2048,48]{0,1:T(8,128)(2,1)S(1)} %collective-permute-done.12), channel_id=1, source_target_pairs={{8,0},{16,8},{24,16},{32,24},{40,32},{48,40},{56,48},{64,56},{72,6... | collective-permute-start | bytes 589832 | tf_op jit(solution)/shard_map/ppermute | solution.py:26
  180.7 9.7 %collective-permute-start.7 = (bf16[2048,48]{0,1:T(8,128)(2,1)S(1)}, bf16[2048,48]{0,1:T(8,128)(2,1)S(1)}, u32[]{:S(2)}, u32[]{:S(2)}) collective-permute-start(bf16[2048,48]{0,1:T(8,128)(2,1)S(1)} %collective-permute-done.6), channel_id=1, source_target_pairs={{0,8},{8,16},{16,24},{24,32},{32,40},{40,48},{48,56},{56,64},{64,7... | collective-permute-start | bytes 589832 | tf_op jit(solution)/shard_map/ppermute | solution.py:24
  184.8 27.0 %collective-permute-start.14 = (bf16[2048,48]{0,1:T(8,128)(2,1)}, bf16[2048,48]{0,1:T(8,128)(2,1)}, u32[]{:S(2)}, u32[]{:S(2)}) collective-permute-start(bf16[2048,48]{0,1:T(8,128)(2,1)} %collective-permute-done.13), channel_id=1, source_target_pairs={{8,0},{16,8},{24,16},{32,24},{40,32},{48,40},{56,48},{64,56},{72,6... | collective-permute-start | bytes 589832 | tf_op jit(solution)/shard_map/ppermute | solution.py:26
  205.0 30.6 %all-to-all-start.3 = ((bf16[16,512,128]{2,1,0:T(8,128)(2,1)}), bf16[16,512,128]{2,1,0:T(8,128)(2,1)}, u32[]{:S(2)}, u32[]{:S(2)}) async-start(bf16[16,512,128]{2,1,0:T(8,128)(2,1)} %gather_fusion.7), calls=%async_computation.3 | async-start | bytes 4194304 | tf_op jit(solution)/shard_map/all_to_all | solution.py:180
  (17 other events, 250.9 us)
Sparse Core Ops, SparseCore 0:
  13.3 47.1 all-gather.2
  74.1 50.4 all-gather.4
